TPU v7x, 32 devices: a whole 2x2x4 slice. The times are simulated.
32 devices in a mesh: dp: 4 (over y, x), expert: 8 (over z, core).
Axes of the slice: x: 2, y: 2, z: 4, core: 2. Of those that a mesh axis runs over, the one named last changes fastest.
Arguments:
- context: bfloat16 [8, 4, 128, 1536], P('expert', None, None, 'dp'), may hold values from -0.29882812 to 0.29882812
- w_proj: bfloat16 [1536, 1536], P('dp'), may hold values from -0.15625 to 0.15625
- residual: bfloat16 [4096, 1536], P(('dp', 'expert')), may hold values from -0.29882812 to 0.29882812
- gain_first: float32 [1536], replicated, may hold values from 0.25 to 1.75
- gain_next: float32 [1536], replicated, may hold values from 0.25 to 1.75
- w_router: bfloat16 [1536, 40], replicated, may hold values from -0.15625 to 0.15625
- expert_ids: int32 [4096, 8], P(('dp', 'expert')), may hold values from 0 to 39, all different within a row
- replica_pick: int32 [4096, 8], P(('dp', 'expert')), may hold values from 0 to 5039
- slot_expert: int32 [48], replicated, may hold values from 0 to 39, as said below
- cap_blocks: int32 [48], replicated, may hold values from 1 to 4
- w_in: bfloat16 [48, 1536, 1024], P('expert', 'dp'), as said below
- w_out: bfloat16 [48, 512, 1536], P('expert', 'dp'), as said below
Outputs:
- residual_out: bfloat16 [4096, 1536], P(('dp', 'expert'))
- next_normed: bfloat16 [4096, 1536], P(('dp', 'expert'))
Inputs may be any that keep to these rules, and one draw needn't show every extreme that they name: `slot_expert`: every expert is held by at least one slot; slot s lies on index s // 6 of the expert axis. `w_in`: two slots that hold the same expert have equal weights. `w_out`: two slots that hold the same expert have equal weights.
All inputs are finite; a program needn't handle non-finite values.
Results may differ from a plain program's by a relative error of at most 0.01.
Values may be sent and summed in bfloat16 or wider, within the bound.
No kernel may reach another device: no remote copies, remote signals or barrier semaphores. Data moves between devices by JAX's collectives and lax.ppermute only.
A program may use at most 128 MiB of HBM per device.

v0:
```python
import jax
import jax.numpy as jnp
from jax import lax
from jax.sharding import PartitionSpec as P

CAP_UNIT = 8
CAP_MOST = 32


def rms_scale(values, gain):
    widened = values.astype(jnp.float32)
    return widened * lax.rsqrt(jnp.mean(widened * widened, axis=-1, keepdims=True) + 1e-06) * gain


def route_rows(
    normed, w_router, expert_ids, replica_pick, slot_expert, cap_blocks, groups, cap_unit
):
    row_count = normed.shape[0]
    experts_all = w_router.shape[1]
    slots_all = slot_expert.shape[0]
    topk_all = expert_ids.shape[1]
    logits = jnp.dot(normed, w_router, preferred_element_type=jnp.float32)
    expert_axis = jnp.arange(experts_all)
    one_hot = expert_ids[:, :, None] == expert_axis
    chosen = jnp.sum(jnp.where(one_hot, logits[:, None, :], jnp.float32(0.0)), axis=-1)
    raised = jnp.exp(chosen)
    gates = raised / jnp.sum(raised, axis=-1, keepdims=True)
    holder = (slot_expert[None, :] == expert_axis[:, None]).astype(jnp.int32)
    rep_count = jnp.sum(holder, axis=1)
    earlier = jnp.cumsum(holder, axis=1) - holder
    slot_rank = jnp.sum(earlier * holder, axis=0)
    count_of = jnp.sum(jnp.where(one_hot, rep_count, 0), axis=-1)
    replica = replica_pick % count_of
    slot_axis = jnp.arange(slots_all)
    matched = (slot_expert == expert_ids[:, :, None]) & (slot_rank == replica[:, :, None])
    target_slot = jnp.sum(jnp.where(matched, slot_axis, 0), axis=-1)
    selected = matched.astype(jnp.int32).reshape(groups, -1, slots_all)
    before = jnp.cumsum(selected, axis=1) - selected
    position = jnp.sum(before * selected, axis=-1).reshape(row_count, topk_all)
    capacity = (
        jnp.sum(jnp.where(target_slot[:, :, None] == slot_axis, cap_blocks, 0), axis=-1) * cap_unit
    )
    retained = position < capacity
    return (gates, target_slot, position, retained)


def on_device(
    context,
    w_proj,
    residual,
    gain_first,
    gain_next,
    w_router,
    expert_ids,
    replica_pick,
    slot_expert,
    cap_blocks,
    w_in,
    w_out,
):
    tok_rows = residual.shape[0]
    model_width = residual.shape[1]
    topk_all = expert_ids.shape[1]
    slots_all = slot_expert.shape[0]
    slot_local = w_in.shape[0]
    expert_count = lax.axis_size("expert")
    full_in, full_out = (
        lax.all_gather(w_in, "dp", axis=1, tiled=True),
        lax.all_gather(w_out, "dp", axis=1, tiled=True),
    )
    hidden_units = full_in.shape[2] // 2
    flat_context = context.reshape(-1, context.shape[3])
    attended = lax.psum_scatter(
        jnp.dot(flat_context, w_proj, preferred_element_type=jnp.float32),
        "dp",
        scatter_dimension=0,
        tiled=True,
    )
    hidden_state = (residual.astype(jnp.float32) + attended).astype(jnp.bfloat16)
    normed = rms_scale(hidden_state, gain_first).astype(jnp.bfloat16)
    gates, target_slot, position, retained = route_rows(
        normed, w_router, expert_ids, replica_pick, slot_expert, cap_blocks, 1, CAP_UNIT
    )
    target = jnp.where(retained, position, CAP_MOST)
    spread_rows = jnp.broadcast_to(normed[:, None, :], (tok_rows, topk_all, model_width))
    outgoing = (
        jnp.zeros((slots_all, CAP_MOST, model_width), jnp.bfloat16)
        .at[target_slot, target]
        .set(spread_rows, mode="drop")
    )
    received = lax.all_to_all(outgoing, "expert", split_axis=0, concat_axis=0, tiled=True)
    received = received.reshape(expert_count, slot_local, CAP_MOST, model_width)
    gate_up = jnp.einsum("jsrd,sdf->jsrf", received, full_in, preferred_element_type=jnp.float32)
    activated = (jax.nn.silu(gate_up[..., :hidden_units]) * gate_up[..., hidden_units:]).astype(
        jnp.bfloat16
    )
    expert_out = jnp.einsum(
        "jsrf,sfd->jsrd", activated, full_out, preferred_element_type=jnp.float32
    ).astype(jnp.bfloat16)
    expert_out = expert_out.reshape(slots_all, CAP_MOST, model_width)
    returned = lax.all_to_all(expert_out, "expert", split_axis=0, concat_axis=0, tiled=True)
    clipped = jnp.minimum(position, CAP_MOST - 1)
    picked = returned[target_slot, clipped]
    weighting = jnp.where(retained, gates, jnp.float32(0.0))
    combined = jnp.sum(weighting[:, :, None] * picked.astype(jnp.float32), axis=1)
    residual_out = (hidden_state.astype(jnp.float32) + combined).astype(jnp.bfloat16)
    next_normed = rms_scale(residual_out, gain_next).astype(jnp.bfloat16)
    return (residual_out, next_normed)


def solution(mesh):
    placed = (
        P("expert", None, None, "dp"),
        P("dp", None),
        P(("dp", "expert"), None),
        P(),
        P(),
        P(),
        P(("dp", "expert"), None),
        P(("dp", "expert"), None),
        P(),
        P(),
        P("expert", "dp", None),
        P("expert", "dp", None),
    )
    return jax.shard_map(
        on_device,
        mesh=mesh,
        in_specs=placed,
        out_specs=(P(("dp", "expert"), None), P(("dp", "expert"), None)),
        check_vma=False,
    )
```

profile of v0, /device:TPU:0, one launch (start us, length us, event | category | flops | bytes accessed | tf_op | source)
XLA Modules:
  0.0 491.6 jit_solution(5937265904727964733)
XLA Ops:
  7.2 0.0 copy-start
  7.2 0.0 reduce-scatter.2.cloned.1.call-start
  7.2 1.2 copy-done
  8.4 3.7 fusion.36
  12.2 0.0 reduce-scatter.2.cloned.1.call-update
  12.2 0.0 copy-start.10
  12.2 0.0 copy-start.12
  12.2 0.0 copy-start.11
  12.2 0.0 copy-start.3
  12.2 0.0 all-gather.3.cloned.1.call-start
  12.3 0.7 all-gather.3.cloned.1.call-update
  13.0 0.0 copy-start.7
  13.0 0.0 all-gather.5.cloned.1.call-start
  13.1 0.7 all-gather.5.cloned.1.call-update
  13.7 0.0 copy-done.5
  13.8 0.1 copy.53
  13.9 0.0 copy-done.6
  13.9 0.2 reduce_window_sum.31
  14.1 0.1 select_reduce_fusion.4
  14.2 0.1 select_reduce_fusion.3
  14.3 0.0 copy-done.9
  14.3 0.1 add_select_fusion
  14.4 0.1 copy.54
  14.5 0.1 eq.117
  14.6 0.1 eq.106
  14.7 0.1 convert_bitcast_fusion.1
  14.9 13.5 %reduce-window.6 = s32[1,48,8,128]{3,2,1,0:T(8,128)S(1)} reduce-window(s32[1,48,8,128]{3,2,1,0:T(8,128)S(1)} %bitcast.57, s32[]{:T(128)} %constant.11.clone.1), window={size=1x1x1x128 pad=0_0x0_0x0_0x127_0}, to_apply=%region_5.6 | reduce-window | flops 6242304 | bytes 393220 | tf_op jit(solution)/shard_map/reduce-window
  28.4 0.1 slice.18
  28.6 0.1 copy.55
  28.7 0.1 copy.56
  28.8 0.1 broadcast.256
  29.0 0.1 fusion.28
  29.1 0.1 reshape.345
  29.2 0.1 select_reduce_fusion.1
  29.4 0.0 copy-done.10
  29.4 0.1 select_reduce_fusion
  29.5 0.1 multiply_reduce_fusion
  29.6 0.1 and_reduce_fusion
  29.7 0.1 copy.61
  29.8 0.1 reshape.358
  29.9 29.2 %reduce-scatter.2.cloned.1.call-done = f32[128,1536]{1,0:T(8,128)} async-done(((f32[512,1536]{1,0:T(8,128)}), f32[128,1536]{1,0:T(8,128)}) %reduce-scatter.2.cloned.1.call-update) | async-done | bytes 786448 | tf_op jit(solution)/shard_map/reduce_scatter | solution.py:73
  59.1 0.0 copy-done.3
  59.1 1.3 fusion.23
  60.4 0.2 fusion.25
  60.6 9.2 %scatter_custom_fusion = bf16[1536,1536]{1,0:T(8,128)(2,1)} fusion(s32[1024]{0:T(1024)S(1)} %reshape.358, bf16[]{:T(256)} %constant.33.clone.1, bf16[128,1536]{1,0:T(8,128)(2,1)S(1)} %fusion.25), kind=kCustom, calls=%fused_computation.12 | custom fusion | bytes 5111810
  69.8 109.9 %all_to_all.10 = bf16[48,32,1536]{2,1,0:T(8,128)(2,1)} all-to-all(bf16[48,32,1536]{2,1,0:T(8,128)(2,1)} %bitcast.54), channel_id=1, replica_groups=mesh['dp'=4,'expert'=8] {'expert'}, dimensions={0} | all-to-all | bytes 9437184 | tf_op jit(solution)/shard_map/all_to_all | solution.py:91
  179.7 56.9 %all-gather.3.cloned.1.call-done = bf16[6,1536,1024]{2,1,0:T(8,128)(2,1)} async-done(((bf16[6,384,1024]{2,1,0:T(8,128)(2,1)}), bf16[6,1536,1024]{2,1,0:T(8,128)(2,1)}) %all-gather.3.cloned.1.call-update) | async-done | bytes 18874384 | tf_op jit(solution)/shard_map/all_gather | solution.py:68
  236.6 12.1 %fusion.11 = f32[8,6,32,1024]{3,2,0,1:T(8,128)} fusion(bf16[6,1536,1024]{2,1,0:T(8,128)(2,1)} %all-gather.3.cloned.1.call-done, bf16[8,6,32,1536]{3,2,1,0:T(8,128)(2,1)} %bitcast.55), kind=kOutput, calls=%fused_computation.14 | convolution fusion | flops 4831838208 | bytes 29884416 | tf_op jit(solution)/shard_map/jsrd,sdf->jsrf/dot_general | solution.py:93
  248.7 86.0 %all-gather.5.cloned.1.call-done = bf16[6,512,1536]{2,1,0:T(8,128)(2,1)} async-done(((bf16[6,128,1536]{2,1,0:T(8,128)(2,1)}), bf16[6,512,1536]{2,1,0:T(8,128)(2,1)}) %all-gather.5.cloned.1.call-update) | async-done | bytes 9437200 | tf_op jit(solution)/shard_map/all_gather | solution.py:69
  334.7 8.2 %convert_bitcast_fusion = bf16[8,6,32,1536]{3,2,0,1:T(8,128)(2,1)S(1)} fusion(bf16[6,512,1536]{2,1,0:T(8,128)(2,1)} %all-gather.5.cloned.1.call-done, f32[8,6,32,1024]{3,2,0,1:T(8,128)} %fusion.11), kind=kOutput, calls=%fused_computation.9 | convolution fusion | flops 2422996992 | bytes 20447232 | tf_op jit(solution)/shard_map/jsrf,sfd->jsrd/dot_general | solution.py:97
  342.9 2.5 copy.63
  345.4 4.9 all-to-all-start.1
  350.3 0.1 reshape.344
  350.4 0.1 copy.65
  350.5 0.1 reshape.352
  350.6 0.2 fusion.37
  350.9 0.1 select_reduce_fusion.2
  351.0 0.1 copy.58
  351.1 104.5 %all-to-all-done.1 = bf16[48,32,1536]{2,1,0:T(8,128)(2,1)} async-done(((bf16[48,32,1536]{2,1,0:T(8,128)(2,1)}), bf16[48,32,1536]{2,1,0:T(8,128)(2,1)}, u32[]{:S(2)}, u32[]{:S(2)}) %all-to-all-start.1) | async-done | bytes 4718624 | tf_op jit(solution)/shard_map/all_to_all | solution.py:101
  455.5 23.6 %gather_fusion = bf16[1024,1536]{1,0:T(8,128)(2,1)} fusion(bf16[48,32,1536]{2,1,0:T(8,128)(2,1)} %all-to-all-done.1, s32[1024]{0:T(1024)S(1)} %reshape.352), kind=kCustom, calls=%fused_computation | custom fusion | bytes 6299648 | tf_op jit(solution)/shard_map/gather | solution.py:103
  479.1 4.7 fusion.4
  483.9 0.2 fusion.20
  484.1 0.9 fusion.22
  485.0 0.0 copy-done.1
  (27 shorter events, 0.3 us)
Async XLA Ops:
  7.2 1.3 copy-start
  7.2 51.9 %reduce-scatter.2.cloned.1.call-start = ((), (), s32[]{:S(2)}) async-start(), calls=%async_computation.3 | async-start | bytes 3932160 | tf_op jit(solution)/shard_map/reduce_scatter | solution.py:73
  12.2 1.6 copy-start.5
  12.2 1.7 copy-start.6
  12.2 2.1 copy-start.9
  12.2 17.2 %copy-start.10 = (s32[48]{0:T(128)S(1)}, s32[48]{0:T(128)}, u32[]{:S(2)}) copy-start(s32[48]{0:T(128)} %param.21) | copy-start | bytes 580
  12.2 17.3 %copy-start.12 = (s32[2]{0:T(128)S(1)}, s32[2]{0:T(128)}, u32[]{:S(2)}) copy-start(s32[2]{0:T(128)} %constant.41) | copy-start | bytes 28
  12.2 17.4 %copy-start.11 = (s32[2]{0:T(128)S(1)}, s32[2]{0:T(128)}, u32[]{:S(2)}) copy-start(s32[2]{0:T(128)} %constant.44) | copy-start | bytes 28
  12.2 46.9 %copy-start.3 = (bf16[128,1536]{1,0:T(8,128)(2,1)S(1)}, bf16[128,1536]{1,0:T(8,128)(2,1)}, u32[]{:S(2)}) copy-start(bf16[128,1536]{1,0:T(8,128)(2,1)} %param.14) | copy-start | bytes 1179652
  12.2 224.4 %all-gather.3.cloned.1.call-start = ((), (), s32[]{:S(2)}) async-start(), calls=%async_computation.4 | async-start | bytes 23592960 | tf_op jit(solution)/shard_map/all_gather | solution.py:68
  13.0 47.4 %copy-start.7 = (f32[1536]{0:T(1024)S(1)}, f32[1536]{0:T(1024)}, u32[]{:S(2)}) copy-start(f32[1536]{0:T(1024)} %param.15) | copy-start | bytes 18436
  13.0 321.7 %all-gather.5.cloned.1.call-start = ((), (), s32[]{:S(2)}) async-start(), calls=%async_computation.5 | async-start | bytes 11796480 | tf_op jit(solution)/shard_map/all_gather | solution.py:69
  345.4 5.2 %copy-start.4 = (bf16[1536,40]{0,1:T(8,128)(2,1)S(1)}, bf16[1536,40]{0,1:T(8,128)(2,1)}, u32[]{:S(2)}) copy-start(bf16[1536,40]{0,1:T(8,128)(2,1)} %param.17) | copy-start | bytes 368644
  345.4 110.1 %all-to-all-start.1 = ((bf16[48,32,1536]{2,1,0:T(8,128)(2,1)}), bf16[48,32,1536]{2,1,0:T(8,128)(2,1)}, u32[]{:S(2)}, u32[]{:S(2)}) async-start(bf16[48,32,1536]{2,1,0:T(8,128)(2,1)} %bitcast.53), calls=%async_computation.2 | async-start | bytes 9437184 | tf_op jit(solution)/shard_map/all_to_all | solution.py:101
  455.5 29.5 %copy-start.1 = (bf16[384,1536]{1,0:T(8,128)(2,1)S(1)}, bf16[384,1536]{1,0:T(8,128)(2,1)}, u32[]{:S(2)}) copy-start(bf16[384,1536]{1,0:T(8,128)(2,1)} %param.13) | copy-start | bytes 3538948
  479.1 5.0 %copy-start.8 = (f32[1536]{0:T(1024)S(1)}, f32[1536]{0:T(1024)}, u32[]{:S(2)}) copy-start(f32[1536]{0:T(1024)} %param.16) | copy-start | bytes 18436
  484.1 0.9 copy-start.2
Sparse Core Ops, SparseCore 0:
  12.3 46.7 reduce-scatter.1
  60.9 175.6 all-gather.2
  238.5 96.1 all-gather.4
where the time goes:
time: 492 us
  waiting for transfers between devices  278 us (57%)
  blocking collectives  110 us (22%)
  local copies, waits for them, and re-layouts  38.3 us (8%)
  matrix products  24.3 us (5%)
  other arithmetic  22.1 us (4%)
  between operations  14 us (3%)
  starting transfers between devices  5.02 us (1%)
    all_to_all x1, blocking collectives, on_device(): lax.all_to_all(outgoing, 'expert', split_axis=0, concat_axis=0, tiled=True)  110 us
    all_to_all x1, waiting for transfers between devices, on_device(): lax.all_to_all(expert_out, 'expert', split_axis=0, concat_axis=0, tiled=T...  104 us
    all_gather x1, waiting for transfers between devices, on_device(): lax.all_gather(w_out, 'dp', axis=1, tiled=True)  86 us
    all_gather x1, waiting for transfers between devices, on_device(): lax.all_gather(w_in, 'dp', axis=1, tiled=True)  56.9 us
    reduce_scatter x1, waiting for transfers between devices, on_device(): lax.psum_scatter(jnp.dot(flat_context, w_proj, preferred_element_type=jnp...  29.2 us
    gather x1, local copies, waits for them, and re-layouts, on_device(): picked = returned[target_slot, clipped]  23.6 us
    another operation x2, other arithmetic  13.5 us
    dot_general x1, matrix products, on_device(): jnp.einsum('jsrd,sdf->jsrf', received, full_in, preferred_element_type=jn...  12.1 us
  transfers between devices with their start and end apart: 4, of which 4 were waited for; matrix products, arithmetic and copies ran while one was open for 8% of the time, Pallas kernels for 0%

commit v1 on v0

--- a/solution.py
+++ b/solution.py
@@ -5,6 +5,17 @@
 
 CAP_UNIT = 8
 CAP_MOST = 32
+
+
+def collect(array, axis, dim):
+    ways = lax.axis_size(axis)
+    pieces = [array]
+    for far in range(1, ways):
+        pieces.append(
+            lax.ppermute(pieces[far - 1], axis, [(d, (d - 1) % ways) for d in range(ways)])
+        )
+    line = jnp.concatenate(pieces, axis=dim)
+    return jnp.roll(line, lax.axis_index(axis) * array.shape[dim], axis=dim)
 
 
 def rms_scale(values, gain):
@@ -64,10 +75,7 @@
     slots_all = slot_expert.shape[0]
     slot_local = w_in.shape[0]
     expert_count = lax.axis_size("expert")
-    full_in, full_out = (
-        lax.all_gather(w_in, "dp", axis=1, tiled=True),
-        lax.all_gather(w_out, "dp", axis=1, tiled=True),
-    )
+    full_in, full_out = (collect(w_in, "dp", 1), lax.all_gather(w_out, "dp", axis=1, tiled=True))
     hidden_units = full_in.shape[2] // 2
     flat_context = context.reshape(-1, context.shape[3])
     attended = lax.psum_scatter(

time: 492 us -> 607 us (1.23)
  waiting for transfers between devices: 278 us -> 429 us
  blocking collectives: 110 us -> 0 us
  local copies, waits for them, and re-layouts: 38.3 us -> 79.4 us
  starting transfers between devices: 5.02 us -> 36.9 us
    ppermute x0 -> x3, waiting for transfers between devices: none -> 292 us  [collect(): lax.ppermute(pieces[far - 1], axis, [(d, (d - 1) % ways) for d in range(w...]
    all_to_all x1 -> x0, blocking collectives: 110 us -> none  [on_device(): lax.all_to_all(outgoing, 'expert', split_axis=0, concat_axis=0, tiled=True)]
    all_gather x1, waiting for transfers between devices: 86 us -> 21.3 us  [on_device(): lax.all_gather(w_out, 'dp', axis=1, tiled=True)]
    all_gather x1 -> x0, waiting for transfers between devices: 56.9 us -> none  [on_device(): lax.all_gather(w_in, 'dp', axis=1, tiled=True)]
    unnamed x31 -> x42, local copies, waits for them, and re-layouts: 10.9 us -> 46.5 us
    ppermute x0 -> x3, starting transfers between devices: none -> 27.3 us  [collect(): lax.ppermute(pieces[far - 1], axis, [(d, (d - 1) % ways) for d in range(w...]
    reduce_scatter x1, waiting for transfers between devices: 29.2 us -> 10.6 us  [on_device(): lax.psum_scatter(jnp.dot(flat_context, w_proj, preferred_element_type=jnp...]
  transfers between devices with their start and end apart: 4 -> 7, of which waited for: 4 -> 6; matrix products, arithmetic and copies ran while one was open for 8% -> 13% of each run, Pallas kernels for 0% -> 0%
where the time goes in v1:
time: 607 us; the launch traced here: 605 us
  waiting for transfers between devices  429 us (71%)
  local copies, waits for them, and re-layouts  79.4 us (13%)
  starting transfers between devices  36.9 us (6%)
  matrix products  24.2 us (4%)
  other arithmetic  22.1 us (4%)
  between operations  14.3 us (2%)
    ppermute x3, waiting for transfers between devices, collect(): lax.ppermute(pieces[far - 1], axis, [(d, (d - 1) % ways) for d in range(w...  292 us
    all_to_all x1, waiting for transfers between devices, on_device(): lax.all_to_all(expert_out, 'expert', split_axis=0, concat_axis=0, tiled=T...  104 us
    unnamed x42, local copies, waits for them, and re-layouts  46.5 us
    ppermute x3, starting transfers between devices, collect(): lax.ppermute(pieces[far - 1], axis, [(d, (d - 1) % ways) for d in range(w...  27.3 us
    gather x1, local copies, waits for them, and re-layouts, on_device(): picked = returned[target_slot, clipped]  23.6 us
    all_gather x1, waiting for transfers between devices, on_device(): lax.all_gather(w_out, 'dp', axis=1, tiled=True)  21.3 us
    another operation x2, other arithmetic  13.5 us
    dot_general x1, matrix products, on_device(): jnp.einsum('jsrd,sdf->jsrf', received, full_in, preferred_element_type=jn...  12.2 us
  transfers between devices with their start and end apart: 7, of which 6 were waited for; matrix products, arithmetic and copies ran while one was open for 13% of the time, Pallas kernels for 0%

profile of v1, /device:TPU:0, one launch (start us, length us, event | category | flops | bytes accessed | tf_op | source)
XLA Modules:
  0.0 605.5 jit_solution(9738321192811187605)
XLA Ops:
  7.2 0.0 copy-start
  7.2 0.0 reduce-scatter.2.cloned.1.call-start
  7.2 1.2 copy-done
  8.5 3.6 fusion.38
  12.1 0.0 reduce-scatter.2.cloned.1.call-update
  12.1 0.0 all-gather.2.cloned.1.call-start
  12.2 4.0 collective-permute-start
  16.2 0.0 all-gather.2.cloned.1.call-update
  16.2 0.1 copy.53
  16.3 0.2 reduce_window_sum.31
  16.5 0.1 select_reduce_fusion.4
  16.6 0.1 select_reduce_fusion.3
  16.8 0.1 add_select_fusion
  16.9 0.1 copy.54
  17.0 0.1 eq.120
  17.1 0.1 eq.109
  17.2 117.2 %collective-permute-done = bf16[6,384,1024]{2,1,0:T(8,128)(2,1)} collective-permute-done((bf16[6,384,1024]{2,1,0:T(8,128)(2,1)}, bf16[6,384,1024]{2,1,0:T(8,128)(2,1)}, u32[]{:S(2)}, u32[]{:S(2)}) %collective-permute-start) | collective-permute-done | bytes 4718624 | tf_op jit(solution)/shard_map/ppermute | solution.py:15
  134.4 3.4 collective-permute-start.1
  137.8 0.1 convert_bitcast_fusion.1
  137.9 13.5 %reduce-window.6 = s32[1,48,8,128]{3,2,1,0:T(8,128)S(1)} reduce-window(s32[1,48,8,128]{3,2,1,0:T(8,128)S(1)} %bitcast.58, s32[]{:T(128)} %constant.48.clone.1), window={size=1x1x1x128 pad=0_0x0_0x0_0x127_0}, to_apply=%region_5.6 | reduce-window | flops 6242304 | bytes 393220 | tf_op jit(solution)/shard_map/reduce-window
  151.4 0.1 slice.18
  151.6 0.1 copy.55
  151.8 0.1 copy.56
  151.8 0.1 broadcast.256
  152.0 0.1 fusion.29
  152.1 0.1 reshape.345
  152.3 0.1 select_reduce_fusion.1
  152.4 0.1 select_reduce_fusion
  152.5 0.1 multiply_reduce_fusion
  152.6 0.1 and_reduce_fusion
  152.7 0.1 copy.61
  152.8 0.1 reshape.358
  152.9 10.6 %reduce-scatter.2.cloned.1.call-done = f32[128,1536]{1,0:T(8,128)} async-done(((f32[512,1536]{1,0:T(8,128)}), f32[128,1536]{1,0:T(8,128)}) %reduce-scatter.2.cloned.1.call-update) | async-done | bytes 786448 | tf_op jit(solution)/shard_map/reduce_scatter | solution.py:81
  163.5 1.3 fusion.24
  164.9 0.2 fusion.26
  165.0 8.3 %scatter_custom_fusion = bf16[1536,1536]{1,0:T(8,128)(2,1)} fusion(s32[1024]{0:T(1024)S(1)} %reshape.358, bf16[]{:T(256)} %constant.58.clone.1, bf16[128,1536]{1,0:T(8,128)(2,1)S(1)} %fusion.26), kind=kCustom, calls=%fused_computation.13 | custom fusion | bytes 5111810
  173.4 4.6 all-to-all-start
  178.0 68.8 %collective-permute-done.1 = bf16[6,384,1024]{2,1,0:T(8,128)(2,1)} collective-permute-done((bf16[6,384,1024]{2,1,0:T(8,128)(2,1)}, bf16[6,384,1024]{2,1,0:T(8,128)(2,1)}, u32[]{:S(2)}, u32[]{:S(2)}) %collective-permute-start.1) | collective-permute-done | bytes 4718624 | tf_op jit(solution)/shard_map/ppermute | solution.py:15
  246.7 20.0 %collective-permute-start.2 = (bf16[6,384,1024]{2,1,0:T(8,128)(2,1)}, bf16[6,384,1024]{2,1,0:T(8,128)(2,1)}, u32[]{:S(2)}, u32[]{:S(2)}) collective-permute-start(bf16[6,384,1024]{2,1,0:T(8,128)(2,1)} %collective-permute-done.1), channel_id=1, source_target_pairs={{0,24},{8,0},{16,8},{24,16},{1,25},{9,1},{17,9},{25,17},{2,26},{10... | collective-permute-start | bytes 14155784 | tf_op jit(solution)/shard_map/ppermute | solution.py:15
  266.7 5.5 constant_dynamic-update-slice_fusion.7
  272.2 5.5 constant_dynamic-update-slice_fusion.6
  277.7 5.6 constant_dynamic-update-slice_fusion.5
  283.4 106.2 %collective-permute-done.2 = bf16[6,384,1024]{2,1,0:T(8,128)(2,1)} collective-permute-done((bf16[6,384,1024]{2,1,0:T(8,128)(2,1)}, bf16[6,384,1024]{2,1,0:T(8,128)(2,1)}, u32[]{:S(2)}, u32[]{:S(2)}) %collective-permute-start.2) | collective-permute-done | bytes 4718624 | tf_op jit(solution)/shard_map/ppermute | solution.py:15
  389.6 5.5 constant_dynamic-update-slice_fusion.4
  395.1 3.2 constant_dynamic-update-slice_fusion.3
  398.4 5.6 constant_dynamic-update-slice_fusion.2
  404.0 5.4 constant_dynamic-update-slice_fusion.1
  409.4 5.5 constant_dynamic-update-slice_fusion
  414.9 12.2 %fusion.12 = f32[8,6,32,1024]{3,2,0,1:T(8,128)} fusion(bf16[8,6,32,1536]{3,2,1,0:T(8,128)(2,1)} %bitcast.11, bf16[6,3072,1024]{2,1,0:T(8,128)(2,1)} %constant_dynamic-update-slice_fusion, s32[]{:T(128)S(6)} %select_n.95), kind=kOutput, calls=%fused_computation.15 | convolution fusion | flops 4831838208 | bytes 29884420 | tf_op jit(solution)/shard_map/jsrd,sdf->jsrf/dot_general | solution.py:101
  427.1 21.3 %all-gather.2.cloned.1.call-done = bf16[6,512,1536]{2,1,0:T(8,128)(2,1)} async-done(((bf16[6,128,1536]{2,1,0:T(8,128)(2,1)}), bf16[6,512,1536]{2,1,0:T(8,128)(2,1)}) %all-gather.2.cloned.1.call-update) | async-done | bytes 9437200 | tf_op jit(solution)/shard_map/all_gather | solution.py:78
  448.4 8.2 %convert_bitcast_fusion = bf16[8,6,32,1536]{3,2,0,1:T(8,128)(2,1)S(1)} fusion(bf16[6,512,1536]{2,1,0:T(8,128)(2,1)} %all-gather.2.cloned.1.call-done, f32[8,6,32,1024]{3,2,0,1:T(8,128)} %fusion.12), kind=kOutput, calls=%fused_computation.10 | convolution fusion | flops 2422996992 | bytes 20447232 | tf_op jit(solution)/shard_map/jsrf,sfd->jsrd/dot_general | solution.py:105
  456.6 2.5 copy.63
  459.1 4.9 all-to-all-start.1
  464.0 0.1 reshape.344
  464.1 0.1 copy.65
  464.2 0.1 reshape.352
  464.4 0.2 fusion.39
  464.6 0.1 select_reduce_fusion.2
  464.7 0.1 copy.58
  464.8 104.3 %all-to-all-done.1 = bf16[48,32,1536]{2,1,0:T(8,128)(2,1)} async-done(((bf16[48,32,1536]{2,1,0:T(8,128)(2,1)}), bf16[48,32,1536]{2,1,0:T(8,128)(2,1)}, u32[]{:S(2)}, u32[]{:S(2)}) %all-to-all-start.1) | async-done | bytes 4718624 | tf_op jit(solution)/shard_map/all_to_all | solution.py:109
  569.1 23.6 %gather_fusion = bf16[1024,1536]{1,0:T(8,128)(2,1)} fusion(bf16[48,32,1536]{2,1,0:T(8,128)(2,1)} %all-to-all-done.1, s32[1024]{0:T(1024)S(1)} %reshape.352), kind=kCustom, calls=%fused_computation | custom fusion | bytes 6299648 | tf_op jit(solution)/shard_map/gather | solution.py:111
  592.8 4.7 fusion.5
  597.5 0.2 fusion.21
  597.7 0.9 fusion.23
  (44 shorter events, 0.4 us)
Async XLA Ops:
  7.2 1.3 copy-start
  7.2 156.3 %reduce-scatter.2.cloned.1.call-start = ((), (), s32[]{:S(2)}) async-start(), calls=%async_computation.3 | async-start | bytes 3932160 | tf_op jit(solution)/shard_map/reduce_scatter | solution.py:81
  8.4 7.7 %copy-start.5 = (s32[128,8]{0,1:T(8,128)S(1)}, s32[128,8]{0,1:T(8,128)}, u32[]{:S(2)}) copy-start(s32[128,8]{0,1:T(8,128)} %param.18) | copy-start | bytes 12292
  8.4 7.9 %copy-start.6 = (s32[48]{0:T(128)S(1)}, s32[48]{0:T(128)}, u32[]{:S(2)}) copy-start(s32[48]{0:T(128)} %param.20) | copy-start | bytes 580
  8.4 8.3 %copy-start.9 = (s32[128,8]{0,1:T(8,128)S(1)}, s32[128,8]{0,1:T(8,128)}, u32[]{:S(2)}) copy-start(s32[128,8]{0,1:T(8,128)} %param.19) | copy-start | bytes 12292
  12.1 140.3 %copy-start.10 = (s32[48]{0:T(128)S(1)}, s32[48]{0:T(128)}, u32[]{:S(2)}) copy-start(s32[48]{0:T(128)} %param.21) | copy-start | bytes 580
  12.1 140.4 %copy-start.12 = (s32[2]{0:T(128)S(1)}, s32[2]{0:T(128)}, u32[]{:S(2)}) copy-start(s32[2]{0:T(128)} %constant.66) | copy-start | bytes 28
  12.1 140.5 %copy-start.11 = (s32[2]{0:T(128)S(1)}, s32[2]{0:T(128)}, u32[]{:S(2)}) copy-start(s32[2]{0:T(128)} %constant.69) | copy-start | bytes 28
  12.1 151.4 %copy-start.3 = (bf16[128,1536]{1,0:T(8,128)(2,1)S(1)}, bf16[128,1536]{1,0:T(8,128)(2,1)}, u32[]{:S(2)}) copy-start(bf16[128,1536]{1,0:T(8,128)(2,1)} %param.14) | copy-start | bytes 1179652
  12.1 152.8 %copy-start.7 = (f32[1536]{0:T(1024)S(1)}, f32[1536]{0:T(1024)}, u32[]{:S(2)}) copy-start(f32[1536]{0:T(1024)} %param.15) | copy-start | bytes 18436
  12.1 436.3 %all-gather.2.cloned.1.call-start = ((), (), s32[]{:S(2)}) async-start(), calls=%async_computation.4 | async-start | bytes 11796480 | tf_op jit(solution)/shard_map/all_gather | solution.py:78
  12.2 122.2 %collective-permute-start = (bf16[6,384,1024]{2,1,0:T(8,128)(2,1)}, bf16[6,384,1024]{2,1,0:T(8,128)(2,1)}, u32[]{:S(2)}, u32[]{:S(2)}) collective-permute-start(bf16[6,384,1024]{2,1,0:T(8,128)(2,1)} %param.22), channel_id=1, source_target_pairs={{0,24},{8,0},{16,8},{24,16},{1,25},{9,1},{17,9},{25,17},{2,26},{10... | collective-permute-start | bytes 14155784 | tf_op jit(solution)/shard_map/ppermute | solution.py:15
  134.4 112.3 %collective-permute-start.1 = (bf16[6,384,1024]{2,1,0:T(8,128)(2,1)}, bf16[6,384,1024]{2,1,0:T(8,128)(2,1)}, u32[]{:S(2)}, u32[]{:S(2)}) collective-permute-start(bf16[6,384,1024]{2,1,0:T(8,128)(2,1)} %collective-permute-done), channel_id=1, source_target_pairs={{0,24},{8,0},{16,8},{24,16},{1,25},{9,1},{17,9},{25,17},{2,26},{10... | collective-permute-start | bytes 14155784 | tf_op jit(solution)/shard_map/ppermute | solution.py:15
  173.4 241.6 %all-to-all-start = ((bf16[48,32,1536]{2,1,0:T(8,128)(2,1)}), bf16[48,32,1536]{2,1,0:T(8,128)(2,1)}, u32[]{:S(2)}, u32[]{:S(2)}) async-start(bf16[48,32,1536]{2,1,0:T(8,128)(2,1)} %bitcast.55), calls=%async_computation.1 | async-start | bytes 9437184 | tf_op jit(solution)/shard_map/all_to_all | solution.py:99
  246.7 142.9 %collective-permute-start.2 = (bf16[6,384,1024]{2,1,0:T(8,128)(2,1)}, bf16[6,384,1024]{2,1,0:T(8,128)(2,1)}, u32[]{:S(2)}, u32[]{:S(2)}) collective-permute-start(bf16[6,384,1024]{2,1,0:T(8,128)(2,1)} %collective-permute-done.1), channel_id=1, source_target_pairs={{0,24},{8,0},{16,8},{24,16},{1,25},{9,1},{17,9},{25,17},{2,26},{10... | collective-permute-start | bytes 14155784 | tf_op jit(solution)/shard_map/ppermute | solution.py:15
  277.7 117.4 %slice-start = ((s8[4718592]{0:T(1024)(128)(4,1)}), s8[4194304]{0:T(1024)(128)(4,1)S(1)}, s32[]{:S(2)}) async-start(s8[4718592]{0:T(1024)(128)(4,1)} %bitcast.53), calls=%async_computation.5 | async-start | bytes 8388608
  283.4 111.7 %slice-start.1 = ((s8[4718592]{0:T(1024)(128)(4,1)}), s8[524288]{0:T(1024)(128)(4,1)S(1)}, s32[]{:S(2)}) async-start(s8[4718592]{0:T(1024)(128)(4,1)} %bitcast.53), calls=%async_computation.6 | async-start | bytes 1048576
  459.1 5.3 copy-start.4
  459.1 110.1 %all-to-all-start.1 = ((bf16[48,32,1536]{2,1,0:T(8,128)(2,1)}), bf16[48,32,1536]{2,1,0:T(8,128)(2,1)}, u32[]{:S(2)}, u32[]{:S(2)}) async-start(bf16[48,32,1536]{2,1,0:T(8,128)(2,1)} %bitcast.56), calls=%async_computation.2 | async-start | bytes 9437184 | tf_op jit(solution)/shard_map/all_to_all | solution.py:109
  569.1 29.5 %copy-start.1 = (bf16[384,1536]{1,0:T(8,128)(2,1)S(1)}, bf16[384,1536]{1,0:T(8,128)(2,1)}, u32[]{:S(2)}) copy-start(bf16[384,1536]{1,0:T(8,128)(2,1)} %param.13) | copy-start | bytes 3538948
  592.8 5.0 copy-start.8
  597.7 0.9 copy-start.2
Sparse Core Ops, SparseCore 0:
  12.3 151.2 reduce-scatter.1
  165.4 282.9 all-gather.1
